TPU v7x, 32 devices: a whole 2x2x4 slice. The times are simulated.
32 devices in a mesh: req: 8 (over z, x), kv: 4 (over y, core).
Axes of the slice: x: 2, y: 2, z: 4, core: 2. Of those that a mesh axis runs over, the one named last changes fastest.
Arguments:
- activations: bfloat16 [4992, 2048], P('req', 'kv'), may hold values from -6 to 6
- span_length: int32 [104], P('req'), may hold values from 1 to 48, as said below
- offsets: int32 [104], P('req'), may hold values from 64 to 8191
- decode_slot: int32 [104], P('req'), may hold values from 0 to 103, as said below
- attention_gain: float32 [2048], replicated, may hold values from 0.1 to 1.9
- query_weight: bfloat16 [2048, 2048], P(None, 'kv'), may hold values from -0.125 to 0.125
- key_projection_matrix: bfloat16 [2048, 1024], P(None, 'kv'), may hold values from -0.125 to 0.125
- value_projection_matrix: bfloat16 [2048, 1024], P(None, 'kv'), may hold values from -0.125 to 0.125
- output_weight: bfloat16 [2048, 2048], P('kv'), may hold values from -0.125 to 0.125
- feedforward_gain: float32 [2048], replicated, may hold values from 0.1 to 1.9
- gate_weight: bfloat16 [2048, 4096], P(None, 'kv'), may hold values from -0.125 to 0.125
- up_weight: bfloat16 [2048, 4096], P(None, 'kv'), may hold values from -0.125 to 0.125
- down_weight: bfloat16 [4096, 2048], P('kv'), may hold values from -0.09375 to 0.09375
- earlier_rotated_keys: bfloat16 [104, 64, 1024], P('req', 'kv'), may hold values from -300 to 300
- earlier_values: bfloat16 [104, 64, 1024], P('req', 'kv'), may hold values from -6 to 6
Outputs:
- layer_out: bfloat16 [4992, 2048], P('req', 'kv')
- decode_keys: bfloat16 [104, 64, 1024], P('req', None, 'kv')
- decode_values: bfloat16 [104, 64, 1024], P('req', None, 'kv')
Inputs may be any that keep to these rules, and one draw needn't show every extreme that they name: `span_length`: on some prefill device every request fills all 48 positions. `decode_slot`: each slot appears once; decode device d owns slots d * 13 to (d + 1) * 13 - 1; at most 2 requests of one prefill device go to one decode device; every prefill device p sends exactly 2 requests to decode device p + 1 (counted round); the differences of decode device minus prefill device, modulo the number of devices of req, form the same multiset on every prefill device.
All inputs are finite; a program needn't handle non-finite values.
Results may differ from a plain program's by a relative error of at most 0.012.
Values may be sent and summed in bfloat16 or wider, within the bound.
No kernel may reach another device: no remote copies, remote signals or barrier semaphores. Data moves between devices by JAX's collectives and lax.ppermute only.
A program may use at most 128 MiB of HBM per device.

v0:
```python
import math
import jax
import jax.numpy as jnp
from jax import lax
from jax.sharding import PartitionSpec as P

HEAD_WIDTH = 256
rope_base = 1000042.0
epsilon = 1e-05


def rms_scale(values, gain_row):
    square_sum = jnp.sum(values * values, axis=-1, keepdims=True)
    return values * lax.rsqrt(square_sum / values.shape[-1] + epsilon) * gain_row


def rotate_pairs(tensor, position):
    half_size = tensor.shape[-1] // 2
    steps_float = jnp.arange(half_size, dtype=jnp.float32)
    inverse = jnp.exp(steps_float * (-2.0 * math.log(rope_base) / tensor.shape[-1]))
    angles = position[:, :, None] * inverse[None, None, :]
    cosine = jnp.cos(angles)[:, :, None, :]
    sine_part = jnp.sin(angles)[:, :, None, :]
    first_half = tensor[..., :half_size]
    second = tensor[..., half_size:]
    return jnp.concatenate(
        [first_half * cosine - second * sine_part, second * cosine + first_half * sine_part],
        axis=-1,
    )


def allowed_keys(span_length, span_size, past_size):
    key_pos = jnp.arange(past_size + span_size, dtype=jnp.int32) - past_size
    query_pos = jnp.arange(span_size, dtype=jnp.int32)
    causal = key_pos[None, :] <= query_pos[:, None]
    live_keys = key_pos[None, None, :] < span_length[:, None, None]
    return (key_pos[None, None, :] < 0) | causal[None, :, :] & live_keys


def local(
    activations,
    span_length,
    offsets,
    decode_slot,
    attention_gain,
    query_weight,
    key_projection_matrix,
    value_projection_matrix,
    output_weight,
    feedforward_gain,
    gate_weight,
    up_weight,
    down_weight,
    earlier_rotated_keys,
    earlier_values,
):
    req_count = lax.axis_size("req")
    kv_index = lax.axis_index("kv")
    req_index = lax.axis_index("req")
    request_list = span_length.shape[0]
    total_rows, width_share = activations.shape
    span_size = total_rows // request_list
    local_kv = key_projection_matrix.shape[1] // HEAD_WIDTH
    local_q = query_weight.shape[1] // HEAD_WIDTH
    query_groups = local_q // local_kv
    x_whole = lax.all_gather(activations, "kv", axis=1, tiled=True)
    x_float = x_whole.astype(jnp.float32)
    normalized_input = rms_scale(x_float, attention_gain).astype(jnp.bfloat16)
    position = (
        offsets[:, None].astype(jnp.float32) + jnp.arange(span_size, dtype=jnp.float32)[None, :]
    )
    query_rows = jnp.dot(
        normalized_input, query_weight, preferred_element_type=jnp.float32
    ).reshape(request_list, span_size, local_q, HEAD_WIDTH)
    query_rows = rotate_pairs(query_rows, position).astype(jnp.bfloat16)
    fresh_keys = jnp.dot(
        normalized_input, key_projection_matrix, preferred_element_type=jnp.float32
    ).reshape(request_list, span_size, local_kv, HEAD_WIDTH)
    fresh_keys = rotate_pairs(fresh_keys, position).astype(jnp.bfloat16)
    fresh_values = (
        jnp.dot(normalized_input, value_projection_matrix, preferred_element_type=jnp.float32)
        .astype(jnp.bfloat16)
        .reshape(request_list, span_size, local_kv, HEAD_WIDTH)
    )
    head_keys, head_values = (
        lax.all_to_all(earlier_rotated_keys, "kv", split_axis=2, concat_axis=1, tiled=True),
        lax.all_to_all(earlier_values, "kv", split_axis=2, concat_axis=1, tiled=True),
    )
    past_size = head_keys.shape[1]
    combined_keys = jnp.concatenate(
        [head_keys.reshape(request_list, past_size, local_kv, HEAD_WIDTH), fresh_keys], axis=1
    )
    combined_values = jnp.concatenate(
        [head_values.reshape(request_list, past_size, local_kv, HEAD_WIDTH), fresh_values], axis=1
    )
    grouped_queries = query_rows.reshape(
        request_list, span_size, local_kv, query_groups, HEAD_WIDTH
    )
    scores = jnp.einsum(
        "rckgd,rskd->rkgcs", grouped_queries, combined_keys, preferred_element_type=jnp.float32
    ) / math.sqrt(HEAD_WIDTH)
    allowed = allowed_keys(span_length, span_size, past_size)[:, None, None, :, :]
    scores = jnp.where(allowed, scores, -jnp.inf)
    weights = jax.nn.softmax(scores, axis=-1).astype(jnp.bfloat16)
    mixed_heads = jnp.einsum(
        "rkgcs,rskd->rckgd", weights, combined_values, preferred_element_type=jnp.float32
    )
    mixed_heads = mixed_heads.astype(jnp.bfloat16).reshape(total_rows, local_q * HEAD_WIDTH)
    head_part = jnp.dot(mixed_heads, output_weight, preferred_element_type=jnp.float32)
    head_total = lax.psum(head_part, "kv")
    residual = x_float + head_total
    normed_two = rms_scale(residual, feedforward_gain).astype(jnp.bfloat16)
    residual_share = lax.dynamic_slice_in_dim(residual, kv_index * width_share, width_share, 1)
    gate_proj = jnp.dot(normed_two, gate_weight, preferred_element_type=jnp.float32)
    upward = jnp.dot(normed_two, up_weight, preferred_element_type=jnp.float32)
    hidden = (jax.nn.silu(gate_proj) * upward).astype(jnp.bfloat16)
    mlp_share = lax.psum_scatter(
        jnp.dot(hidden, down_weight, preferred_element_type=jnp.float32),
        "kv",
        scatter_dimension=1,
        tiled=True,
    )
    live_rows = (jnp.arange(span_size, dtype=jnp.int32)[None, :] < span_length[:, None]).reshape(
        total_rows
    )
    layer_out = jnp.where(live_rows[:, None], residual_share + mlp_share, 0.0).astype(jnp.bfloat16)
    slot_table = lax.all_gather(decode_slot, "req", axis=0, tiled=True)
    capacity = max(2, (request_list + req_count - 1) // req_count)
    order_ids = jnp.arange(request_list, dtype=jnp.int32)
    earlier = order_ids[None, :] < order_ids[:, None]
    own_dest = decode_slot // request_list
    same_dest = own_dest[:, None] == own_dest[None, :]
    own_rank = jnp.sum((same_dest & earlier).astype(jnp.int32), axis=1)
    buffer_place = own_dest * capacity + own_rank
    buffer_ids = jnp.arange(req_count * capacity, dtype=jnp.int32)
    matches = buffer_place[None, :] == buffer_ids[:, None]
    picked = jnp.sum(jnp.where(matches, order_ids[None, :], 0), axis=1)
    filled = jnp.any(matches, axis=1)

    def pack_slots(source_cache):
        taken_rows = jnp.take(source_cache, picked, axis=0)
        taken_rows = jnp.where(filled[:, None, None], taken_rows, jnp.zeros((), source_cache.dtype))
        return taken_rows.reshape((req_count, capacity) + source_cache.shape[1:])

    arrived_keys, arrived_values = (
        lax.all_to_all(pack_slots(head_keys), "req", split_axis=0, concat_axis=0, tiled=True),
        lax.all_to_all(pack_slots(head_values), "req", split_axis=0, concat_axis=0, tiled=True),
    )
    all_dest = (slot_table // request_list).reshape(req_count, request_list)
    same_all = all_dest[:, :, None] == all_dest[:, None, :]
    rank_all = jnp.sum((same_all & earlier[None, :, :]).astype(jnp.int32), axis=2).reshape(-1)
    wanted = req_index * request_list + order_ids
    slot_hits = slot_table[None, :] == wanted[:, None]
    global_ids = jnp.arange(slot_table.shape[0], dtype=jnp.int32)
    source = jnp.sum(jnp.where(slot_hits, global_ids[None, :], 0), axis=1)
    source_rank = jnp.sum(jnp.where(slot_hits, rank_all[None, :], 0), axis=1)
    slot_position = source // request_list * capacity + source_rank
    flat_keys = arrived_keys.reshape((req_count * capacity,) + arrived_keys.shape[2:])
    flat_values = arrived_values.reshape((req_count * capacity,) + arrived_values.shape[2:])
    decode_keys = jnp.take(flat_keys, slot_position, axis=0)
    decode_values = jnp.take(flat_values, slot_position, axis=0)
    return (layer_out, decode_keys, decode_values)


def solution(mesh):
    return jax.shard_map(
        local,
        mesh=mesh,
        in_specs=(
            P("req", "kv"),
            P("req"),
            P("req"),
            P("req"),
            P(),
            P(None, "kv"),
            P(None, "kv"),
            P(None, "kv"),
            P("kv", None),
            P(),
            P(None, "kv"),
            P(None, "kv"),
            P("kv", None),
            P("req", "kv", None),
            P("req", "kv", None),
        ),
        out_specs=(P("req", "kv"), P("req", None, "kv"), P("req", None, "kv")),
        check_vma=False,
    )
```

profile of v0, /device:TPU:0, one launch (start us, length us, event | category | flops | bytes accessed | tf_op | source)
XLA Modules:
  0.0 270.3 jit_solution(3733439131479229272)
XLA Ops:
  7.9 5.7 %copy.36 = bf16[13,16,1024]{1,0,2:T(8,128)(2,1)} copy(bf16[13,16,1024]{2,1,0:T(8,128)(2,1)} %param.32) | data formatting | bytes 851968 | tf_op args[13]
  13.6 5.5 %reshape.332 = bf16[4,2,26624]{2,1,0:T(2,128)(2,1)} reshape(bf16[1024,13,16]{2,1,0:T(8,128)(2,1)} %bitcast.64) | data formatting | bytes 851968
  19.1 4.3 %all-to-all-start.1 = ((bf16[4,2,26624]{2,1,0:T(2,128)(2,1)}), bf16[4,2,26624]{2,1,0:T(2,128)(2,1)S(1)}, u32[]{:S(2)}, u32[]{:S(2)}) async-start(bf16[4,2,26624]{2,1,0:T(2,128)(2,1)} %reshape.332), calls=%async_computation.1 | async-start | bytes 851968 | tf_op jit(solution)/shard_map/all_to_all | solution.py:86
  23.4 4.7 %copy.34 = bf16[13,16,1024]{1,0,2:T(8,128)(2,1)} copy(bf16[13,16,1024]{2,1,0:T(8,128)(2,1)S(1)} %copy-done.9) | data formatting | bytes 851968 | tf_op args[14]
  28.2 5.5 %reshape.330 = bf16[4,2,26624]{2,1,0:T(2,128)(2,1)} reshape(bf16[1024,13,16]{2,1,0:T(8,128)(2,1)} %bitcast.65) | data formatting | bytes 851968
  33.9 2.3 all-to-all-done.1
  36.2 3.5 %all-to-all-start = ((bf16[4,2,26624]{2,1,0:T(2,128)(2,1)}), bf16[4,2,26624]{2,1,0:T(2,128)(2,1)S(1)}, u32[]{:S(2)}, u32[]{:S(2)}) async-start(bf16[4,2,26624]{2,1,0:T(2,128)(2,1)} %reshape.330), calls=%async_computation | async-start | bytes 851968 | tf_op jit(solution)/shard_map/all_to_all | solution.py:87
  39.7 2.0 multiply_cosine_fusion
  41.8 4.4 %reshape.333 = bf16[1024,13,16]{2,1,0:T(8,128)(2,1)} reshape(bf16[4,2,26624]{2,1,0:T(2,128)(2,1)S(1)} %all-to-all-done.1) | data formatting | bytes 851968
  46.2 5.2 %copy.37 = bf16[13,16,4,256]{3,1,2,0:T(8,128)(2,1)} copy(bf16[13,16,4,256]{1,0,3,2:T(8,128)(2,1)} %bitcast.62) | data formatting | bytes 851968 | tf_op jit(solution)/shard_map/all_to_all | solution.py:86
  51.3 4.4 %reshape.331 = bf16[1024,13,16]{2,1,0:T(8,128)(2,1)} reshape(bf16[4,2,26624]{2,1,0:T(2,128)(2,1)S(1)} %all-to-all-done) | data formatting | bytes 851968
  55.7 5.2 %copy.35 = bf16[13,16,4,256]{3,1,2,0:T(8,128)(2,1)} copy(bf16[13,16,4,256]{1,0,3,2:T(8,128)(2,1)} %bitcast.63) | data formatting | bytes 851968 | tf_op jit(solution)/shard_map/all_to_all | solution.py:87
  60.9 2.4 fusion
  63.4 4.2 %fusion.34 = f32[624,512]{1,0:T(8,128)} fusion(bf16[2048,512]{1,0:T(8,128)(2,1)} %param.24, bf16[624,2048]{1,0:T(8,128)(2,1)S(1)} %copy-done.2, f32[2048]{0:T(1024)S(1)} %copy-done.13, f32[624]{0:T(1024)S(1)} %add_rsqrt_fusion.1), kind=kOutput, calls=%fused_computation.90 | convolution fusion | flops 1313734656 | bytes 5941696 | tf_op jit(solution)/shard_map/dot_general | solution.py:72
  67.6 2.1 reshape.272
  70.4 2.9 %fusion.36 = f32[624,256]{1,0:T(8,128)S(1)} fusion(bf16[2048,256]{1,0:T(8,128)(2,1)} %param.25, bf16[624,2048]{1,0:T(8,128)(2,1)} %all-gather.2.cloned.1.call-done, f32[2048]{0:T(1024)S(1)} %copy-done.13, f32[624]{0:T(1024)S(1)} %add_rsqrt_fusion.1), kind=kOutput, calls=%fused_computation.91 | convolution fusion | flops 659423232 | bytes 4254144 | tf_op jit(solution)/shard_map/dot_general | solution.py:76
  73.3 1.6 fusion.22
  77.2 0.9 convolution_convert_fusion.1
  79.4 3.8 %fusion.41 = f32[624,2048]{1,0:T(8,128)} fusion(bf16[624,512]{1,0:T(8,128)(2,1)S(1)} %bitcast.66, bf16[512,2048]{1,0:T(8,128)(2,1)S(1)} %copy-done), kind=kOutput, calls=%fused_computation.94 | convolution fusion | flops 1308622848 | bytes 7847936 | tf_op jit(solution)/shard_map/dot_general | solution.py:109
  83.3 102.7 %all-reduce.3.cloned.1.call-done = f32[624,2048]{1,0:T(8,128)} async-done(((f32[624,2048]{1,0:T(8,128)}), f32[624,2048]{1,0:T(8,128)}) %all-reduce.3.cloned.1.call-update) | async-done | bytes 5111824 | tf_op jit(solution)/shard_map/psum | solution.py:110
  186.0 4.1 %multiply_reduce_fusion = (f32[624]{0:T(1024)S(1)}, f32[624,2048]{1,0:T(8,128)S(1)}) fusion(f32[624,2048]{1,0:T(8,128)} %all-reduce.3.cloned.1.call-done, bf16[624,2048]{1,0:T(8,128)(2,1)} %all-gather.2.cloned.1.call-done), kind=kLoop, calls=%fused_computation.11 | loop fusion | flops 5111184 | bytes 12782016 | tf_op jit(solution)/shard_map/reduce_sum | solution.py:13
  190.1 2.3 copy-done.4
  192.4 4.4 %fusion.33 = f32[624,1024]{1,0:T(8,128)} fusion(bf16[2048,1024]{1,0:T(8,128)(2,1)S(1)} %copy-done.11, f32[624,2048]{1,0:T(8,128)S(1)} %get-tuple-element.10, f32[2048]{0:T(1024)S(1)} %copy-done.14, f32[624]{0:T(1024)S(1)} %add_rsqrt_fusion), kind=kOutput, calls=%fused_computation.89 | convolution fusion | flops 2621079552 | bytes 11872704 | tf_op jit(solution)/shard_map/dot_general | solution.py:114
  196.8 13.5 %fusion.12 = f32[624,2048]{1,0:T(8,128)} fusion(bf16[1024,2048]{1,0:T(8,128)(2,1)} %param.31, f32[624,1024]{1,0:T(8,128)} %fusion.33, bf16[2048,1024]{1,0:T(8,128)(2,1)} %param.30, f32[624,2048]{1,0:T(8,128)} %copy-done.4, f32[2048]{0:T(1024)S(1)} %copy-done.14, f32[624]{0:T(1024)S(1)} %add_rsqrt_fusion), kind=kOutput, calls=%fused_computation.28 | convolution fusion | flops 5242159104 | bytes 21178816 | tf_op jit(solution)/shard_map/dot_general | solution.py:118
  212.6 1.2 select_select_fusion
  213.7 5.5 %all-to-all-start.2 = ((bf16[8,2,64,256]{3,2,1,0:T(8,128)(2,1)}), bf16[8,2,64,256]{3,2,1,0:T(8,128)(2,1)S(1)}, u32[]{:S(2)}, u32[]{:S(2)}) async-start(bf16[8,2,64,256]{3,2,1,0:T(8,128)(2,1)} %bitcast.21), calls=%async_computation.3 | async-start | bytes 1048576 | tf_op jit(solution)/shard_map/all_to_all | solution.py:146
  220.9 13.1 %all-reduce = s32[104]{0:T(128)S(1)} all-reduce(s32[104]{0:T(128)S(1)} %dynamic-update-slice), channel_id=1, replica_groups=mesh['req'=8,'kv'=4] {'req'}, use_global_device_ids=true, to_apply=%add | all-reduce | flops 104 | bytes 832
  234.0 3.5 %all-to-all-start.3 = ((bf16[8,2,64,256]{3,2,1,0:T(8,128)(2,1)}), bf16[8,2,64,256]{3,2,1,0:T(8,128)(2,1)S(1)}, u32[]{:S(2)}, u32[]{:S(2)}) async-start(bf16[8,2,64,256]{3,2,1,0:T(8,128)(2,1)} %bitcast.24), calls=%async_computation.4 | async-start | bytes 1048576 | tf_op jit(solution)/shard_map/all_to_all | solution.py:147
  239.1 12.9 %all-to-all-done.3 = bf16[8,2,64,256]{3,2,1,0:T(8,128)(2,1)S(1)} async-done(((bf16[8,2,64,256]{3,2,1,0:T(8,128)(2,1)}), bf16[8,2,64,256]{3,2,1,0:T(8,128)(2,1)S(1)}, u32[]{:S(2)}, u32[]{:S(2)}) %all-to-all-start.3) | async-done | bytes 524320 | tf_op jit(solution)/shard_map/all_to_all | solution.py:147
  252.6 1.0 broadcast_select_fusion
  253.6 7.5 %reduce-scatter.2.cloned.1.call-done = f32[624,512]{1,0:T(8,128)} async-done(((f32[624,2048]{1,0:T(8,128)}), f32[624,512]{1,0:T(8,128)}) %reduce-scatter.2.cloned.1.call-update) | async-done | bytes 1277968 | tf_op jit(solution)/shard_map/reduce_scatter | solution.py:117
  261.1 2.7 select_convert_fusion
  (89 shorter events, 10.7 us)
Async XLA Ops:
  7.2 72.2 %copy-start = (bf16[512,2048]{1,0:T(8,128)(2,1)S(1)}, bf16[512,2048]{1,0:T(8,128)(2,1)}, u32[]{:S(2)}) copy-start(bf16[512,2048]{1,0:T(8,128)(2,1)} %param.27) | copy-start | bytes 6291460
  7.2 53.7 %all-gather.2.cloned.1.call-start = ((), (), s32[]{:S(2)}) async-start(), calls=%async_computation.5 | async-start | bytes 3194880 | tf_op jit(solution)/shard_map/all_gather | solution.py:66
  13.6 9.8 %copy-start.15 = (s32[13]{0:T(128)S(1)}, s32[13]{0:T(128)}, u32[]{:S(2)}) copy-start(s32[13]{0:T(128)} %param.21) | copy-start | bytes 160
  13.6 9.8 %copy-start.9 = (bf16[13,16,1024]{2,1,0:T(8,128)(2,1)S(1)}, bf16[13,16,1024]{2,1,0:T(8,128)(2,1)}, u32[]{:S(2)}) copy-start(bf16[13,16,1024]{2,1,0:T(8,128)(2,1)} %param.33) | copy-start | bytes 1277956
  19.1 17.1 %all-to-all-start.1 = ((bf16[4,2,26624]{2,1,0:T(2,128)(2,1)}), bf16[4,2,26624]{2,1,0:T(2,128)(2,1)S(1)}, u32[]{:S(2)}, u32[]{:S(2)}) async-start(bf16[4,2,26624]{2,1,0:T(2,128)(2,1)} %reshape.332), calls=%async_computation.1 | async-start | bytes 851968 | tf_op jit(solution)/shard_map/all_to_all | solution.py:86
  28.2 5.5 %copy-start.10 = (s32[13]{0:T(128)S(1)}, s32[13]{0:T(128)}, u32[]{:S(2)}) copy-start(s32[13]{0:T(128)} %param.20) | copy-start | bytes 160
  36.2 15.1 %all-to-all-start = ((bf16[4,2,26624]{2,1,0:T(2,128)(2,1)}), bf16[4,2,26624]{2,1,0:T(2,128)(2,1)S(1)}, u32[]{:S(2)}, u32[]{:S(2)}) async-start(bf16[4,2,26624]{2,1,0:T(2,128)(2,1)} %reshape.330), calls=%async_computation | async-start | bytes 851968 | tf_op jit(solution)/shard_map/all_to_all | solution.py:87
  39.7 146.3 %all-reduce.3.cloned.1.call-start = ((), (), s32[]{:S(2)}) async-start(), calls=%async_computation.6 | async-start | bytes 10223616 | tf_op jit(solution)/shard_map/psum | solution.py:110
  55.7 7.7 %copy-start.13 = (f32[2048]{0:T(1024)S(1)}, f32[2048]{0:T(1024)}, u32[]{:S(2)}) copy-start(f32[2048]{0:T(1024)} %param.23) | copy-start | bytes 24580
  60.9 2.5 copy-start.2
  70.4 4.6 %copy-start.7 = (f32[13,48,128]{2,1,0:T(8,128)S(1)}, f32[13,48,128]{2,1,0:T(8,128)}, u32[]{:S(2)}) copy-start(f32[13,48,128]{2,1,0:T(8,128)} %get-tuple-element.17) | copy-start | bytes 958468
  70.4 4.6 %copy-start.8 = (f32[13,48,128]{2,1,0:T(8,128)S(1)}, f32[13,48,128]{2,1,0:T(8,128)}, u32[]{:S(2)}) copy-start(f32[13,48,128]{2,1,0:T(8,128)} %get-tuple-element.18) | copy-start | bytes 958468
  73.3 1.8 copy-start.5
  75.2 1.7 copy-start.3
  75.2 2.0 copy-start.12
  77.1 1.0 copy-start.6
  83.2 109.2 %copy-start.14 = (f32[2048]{0:T(1024)S(1)}, f32[2048]{0:T(1024)}, u32[]{:S(2)}) copy-start(f32[2048]{0:T(1024)} %param.28) | copy-start | bytes 24580
  83.2 177.9 %reduce-scatter.2.cloned.1.call-start = ((), (), s32[]{:S(2)}) async-start(), calls=%async_computation.7 | async-start | bytes 6389760 | tf_op jit(solution)/shard_map/reduce_scatter | solution.py:117
  186.0 6.4 %copy-start.11 = (bf16[2048,1024]{1,0:T(8,128)(2,1)S(1)}, bf16[2048,1024]{1,0:T(8,128)(2,1)}, u32[]{:S(2)}) copy-start(bf16[2048,1024]{1,0:T(8,128)(2,1)} %param.29) | copy-start | bytes 12582916
  190.1 2.3 copy-start.4
  210.2 0.7 copy-start.16
  211.4 8.0 %copy-start.17 = (u32[32]{0:T(128)S(1)}, u32[32]{0:T(128)}, u32[]{:S(2)}) copy-start(u32[32]{0:T(128)} %constant.89) | copy-start | bytes 388
  213.7 20.2 %all-to-all-start.2 = ((bf16[8,2,64,256]{3,2,1,0:T(8,128)(2,1)}), bf16[8,2,64,256]{3,2,1,0:T(8,128)(2,1)S(1)}, u32[]{:S(2)}, u32[]{:S(2)}) async-start(bf16[8,2,64,256]{3,2,1,0:T(8,128)(2,1)} %bitcast.21), calls=%async_computation.3 | async-start | bytes 1048576 | tf_op jit(solution)/shard_map/all_to_all | solution.py:146
  234.0 18.0 %all-to-all-start.3 = ((bf16[8,2,64,256]{3,2,1,0:T(8,128)(2,1)}), bf16[8,2,64,256]{3,2,1,0:T(8,128)(2,1)S(1)}, u32[]{:S(2)}, u32[]{:S(2)}) async-start(bf16[8,2,64,256]{3,2,1,0:T(8,128)(2,1)} %bitcast.24), calls=%async_computation.4 | async-start | bytes 1048576 | tf_op jit(solution)/shard_map/all_to_all | solution.py:147
  252.0 11.8 %copy-start.1 = (bf16[512,2048]{1,0:T(8,128)(2,1)S(1)}, bf16[512,2048]{1,0:T(8,128)(2,1)}, u32[]{:S(2)}) copy-start(bf16[512,2048]{1,0:T(8,128)(2,1)} %param.27) | copy-start | bytes 6291460
Sparse Core Ops, SparseCore 0:
  9.6 32.4 all-gather.1
  83.3 102.5 all-reduce.2
  210.4 50.6 reduce-scatter.1
where the time goes:
time: 271 us; the launch traced here: 270 us
  waiting for transfers between devices  126 us (46%)
  local copies, waits for them, and re-layouts  51.6 us (19%)
  matrix products  30.7 us (11%)
  other arithmetic  17.2 us (6%)
  starting transfers between devices  16.9 us (6%)
  between operations  14.7 us (5%)
  blocking collectives  13.1 us (5%)
    psum x1, waiting for transfers between devices, local(): head_total = lax.psum(head_part, 'kv')  103 us
    unnamed x46, local copies, waits for them, and re-layouts  35.2 us
    dot_general x1, matrix products, local(): jnp.dot(hidden, down_weight, preferred_element_type=jnp.float32)  13.5 us
    unnamed x1, blocking collectives  13.1 us
    all_to_all x1, waiting for transfers between devices, local(): lax.all_to_all(pack_slots(head_values), 'req', split_axis=0, concat_axis=...  12.9 us
    reduce_scatter x1, waiting for transfers between devices, local(): lax.psum_scatter(jnp.dot(hidden, down_weight, preferred_element_type=jnp....  7.52 us
    reduce_sum x2, other arithmetic, rms_scale(): square_sum = jnp.sum(values * values, axis=-1, keepdims=True)  6.58 us
    all_to_all x1, starting transfers between devices, local(): lax.all_to_all(pack_slots(head_keys), 'req', split_axis=0, concat_axis=0,...  5.5 us
  transfers between devices with their start and end apart: 7, of which 4 were waited for; matrix products, arithmetic and copies ran while one was open for 18% of the time, Pallas kernels for 0%

commit v1 on v0

--- a/solution.py
+++ b/solution.py
@@ -84,7 +84,12 @@
     )
     head_keys, head_values = (
         lax.all_to_all(earlier_rotated_keys, "kv", split_axis=2, concat_axis=1, tiled=True),
-        lax.all_to_all(earlier_values, "kv", split_axis=2, concat_axis=1, tiled=True),
+        jnp.concatenate(
+            lax.all_to_all(
+                jnp.stack(jnp.split(earlier_values, lax.axis_size("kv"), axis=2)), "kv", 0, 0
+            ),
+            axis=1,
+        ),
     )
     past_size = head_keys.shape[1]
     combined_keys = jnp.concatenate(

time: 271 us -> 262 us (0.967)
  local copies, waits for them, and re-layouts: 51.6 us -> 32.9 us
  waiting for transfers between devices: 126 us -> 135 us
    unnamed x46 -> x43, local copies, waits for them, and re-layouts: 35.2 us -> 20.9 us
    all_to_all x1, waiting for transfers between devices: 2.32 us -> 11.7 us  [local(): lax.all_to_all(earlier_rotated_keys, 'kv', split_axis=2, concat_axis=1, t...]
    all_to_all x1, local copies, waits for them, and re-layouts: 5.19 us -> 0.8 us  [local(): lax.all_to_all(jnp.stack(jnp.split(earlier_values, lax.axis_size('kv'), a...]
  transfers between devices with their start and end apart: 7 -> 7, of which waited for: 4 -> 4; matrix products, arithmetic and copies ran while one was open for 18% -> 12% of each run, Pallas kernels for 0% -> 0%
where the time goes in v1:
time: 262 us; the launch traced here: 261 us
  waiting for transfers between devices  135 us (52%)
  local copies, waits for them, and re-layouts  32.9 us (13%)
  matrix products  29.9 us (11%)
  other arithmetic  17.8 us (7%)
  starting transfers between devices  17.1 us (7%)
  between operations  14.7 us (6%)
  blocking collectives  13.1 us (5%)
    psum x1, waiting for transfers between devices, local(): head_total = lax.psum(head_part, 'kv')  103 us
    unnamed x43, local copies, waits for them, and re-layouts  20.9 us
    dot_general x1, matrix products, local(): jnp.dot(hidden, down_weight, preferred_element_type=jnp.float32)  13.5 us
    unnamed x1, blocking collectives  13.1 us
    all_to_all x1, waiting for transfers between devices, local(): lax.all_to_all(pack_slots(head_values), 'req', split_axis=0, concat_axis=...  12.9 us
    all_to_all x1, waiting for transfers between devices, local(): lax.all_to_all(earlier_rotated_keys, 'kv', split_axis=2, concat_axis=1, t...  11.7 us
    reduce_scatter x1, waiting for transfers between devices, local(): lax.psum_scatter(jnp.dot(hidden, down_weight, preferred_element_type=jnp....  7.53 us
    reduce_sum x2, other arithmetic, rms_scale(): square_sum = jnp.sum(values * values, axis=-1, keepdims=True)  6.58 us
  transfers between devices with their start and end apart: 7, of which 4 were waited for; matrix products, arithmetic and copies ran while one was open for 12% of the time, Pallas kernels for 0%

profile of v1, /device:TPU:0, one launch (start us, length us, event | category | flops | bytes accessed | tf_op | source)
XLA Modules:
  0.0 260.9 jit_solution(10607402509292271279)
XLA Ops:
  7.9 5.7 %copy.33 = bf16[13,16,1024]{1,0,2:T(8,128)(2,1)} copy(bf16[13,16,1024]{2,1,0:T(8,128)(2,1)} %param.32) | data formatting | bytes 851968 | tf_op args[13]
  13.6 5.5 %reshape.333 = bf16[4,2,26624]{2,1,0:T(2,128)(2,1)} reshape(bf16[1024,13,16]{2,1,0:T(8,128)(2,1)} %bitcast.68) | data formatting | bytes 851968
  19.1 4.3 %all-to-all-start.1 = ((bf16[4,2,26624]{2,1,0:T(2,128)(2,1)}), bf16[4,2,26624]{2,1,0:T(2,128)(2,1)S(1)}, u32[]{:S(2)}, u32[]{:S(2)}) async-start(bf16[4,2,26624]{2,1,0:T(2,128)(2,1)} %reshape.333), calls=%async_computation.1 | async-start | bytes 851968 | tf_op jit(solution)/shard_map/all_to_all | solution.py:86
  23.5 0.8 pad_maximum_fusion
  24.5 11.7 %all-to-all-done.1 = bf16[4,2,26624]{2,1,0:T(2,128)(2,1)S(1)} async-done(((bf16[4,2,26624]{2,1,0:T(2,128)(2,1)}), bf16[4,2,26624]{2,1,0:T(2,128)(2,1)S(1)}, u32[]{:S(2)}, u32[]{:S(2)}) %all-to-all-start.1) | async-done | bytes 426016 | tf_op jit(solution)/shard_map/all_to_all | solution.py:86
  36.2 3.5 %all-to-all-start = ((bf16[4,13,16,256]{3,2,1,0:T(8,128)(2,1)}), bf16[4,13,16,256]{3,2,1,0:T(8,128)(2,1)S(1)}, u32[]{:S(2)}, u32[]{:S(2)}) async-start(bf16[4,13,16,256]{3,2,1,0:T(8,128)(2,1)} %pad_maximum_fusion), calls=%async_computation | async-start | bytes 851968 | tf_op jit(solution)/shard_map/all_to_all | solution.py:88
  39.7 2.0 multiply_cosine_fusion
  41.8 4.4 %reshape.334 = bf16[1024,13,16]{2,1,0:T(8,128)(2,1)} reshape(bf16[4,2,26624]{2,1,0:T(2,128)(2,1)S(1)} %all-to-all-done.1) | data formatting | bytes 851968
  46.1 5.2 %copy.34 = bf16[13,16,4,256]{3,1,2,0:T(8,128)(2,1)} copy(bf16[13,16,4,256]{1,0,3,2:T(8,128)(2,1)} %bitcast.67) | data formatting | bytes 851968 | tf_op jit(solution)/shard_map/all_to_all | solution.py:86
  51.3 0.8 copy.32
  52.1 2.4 fusion
  54.6 4.2 %fusion.34 = f32[624,512]{1,0:T(8,128)} fusion(bf16[2048,512]{1,0:T(8,128)(2,1)} %param.24, bf16[624,2048]{1,0:T(8,128)(2,1)S(1)} %copy-done.2, f32[2048]{0:T(1024)S(1)} %copy-done.13, f32[624]{0:T(1024)S(1)} %add_rsqrt_fusion.1), kind=kOutput, calls=%fused_computation.95 | convolution fusion | flops 1313734656 | bytes 5941696 | tf_op jit(solution)/shard_map/dot_general | solution.py:72
  58.8 2.1 reshape.274
  60.9 0.7 fusion.39
  61.6 1.0 copy-done.3
  62.6 2.2 fusion.36
  64.8 1.4 fusion.22
  67.7 0.9 convolution_convert_fusion.1
  69.9 3.8 %fusion.41 = f32[624,2048]{1,0:T(8,128)} fusion(bf16[624,512]{1,0:T(8,128)(2,1)S(1)} %bitcast.69, bf16[512,2048]{1,0:T(8,128)(2,1)S(1)} %copy-done), kind=kOutput, calls=%fused_computation.99 | convolution fusion | flops 1308622848 | bytes 7847936 | tf_op jit(solution)/shard_map/dot_general | solution.py:114
  74.0 102.5 %all-reduce.3.cloned.1.call-done = f32[624,2048]{1,0:T(8,128)} async-done(((f32[624,2048]{1,0:T(8,128)}), f32[624,2048]{1,0:T(8,128)}) %all-reduce.3.cloned.1.call-update) | async-done | bytes 5111824 | tf_op jit(solution)/shard_map/psum | solution.py:115
  176.5 4.1 %multiply_reduce_fusion = (f32[624]{0:T(1024)S(1)}, f32[624,2048]{1,0:T(8,128)S(1)}) fusion(f32[624,2048]{1,0:T(8,128)} %all-reduce.3.cloned.1.call-done, bf16[624,2048]{1,0:T(8,128)(2,1)} %all-gather.2.cloned.1.call-done), kind=kLoop, calls=%fused_computation.11 | loop fusion | flops 5111184 | bytes 12782016 | tf_op jit(solution)/shard_map/reduce_sum | solution.py:13
  180.7 2.3 copy-done.4
  182.9 4.4 %fusion.33 = f32[624,1024]{1,0:T(8,128)} fusion(bf16[2048,1024]{1,0:T(8,128)(2,1)S(1)} %copy-done.11, f32[624,2048]{1,0:T(8,128)S(1)} %get-tuple-element.10, f32[2048]{0:T(1024)S(1)} %copy-done.14, f32[624]{0:T(1024)S(1)} %add_rsqrt_fusion), kind=kOutput, calls=%fused_computation.94 | convolution fusion | flops 2621079552 | bytes 11872704 | tf_op jit(solution)/shard_map/dot_general | solution.py:119
  187.3 13.5 %fusion.12 = f32[624,2048]{1,0:T(8,128)} fusion(bf16[1024,2048]{1,0:T(8,128)(2,1)} %param.31, f32[624,1024]{1,0:T(8,128)} %fusion.33, bf16[2048,1024]{1,0:T(8,128)(2,1)} %param.30, f32[624,2048]{1,0:T(8,128)} %copy-done.4, f32[2048]{0:T(1024)S(1)} %copy-done.14, f32[624]{0:T(1024)S(1)} %add_rsqrt_fusion), kind=kOutput, calls=%fused_computation.28 | convolution fusion | flops 5242159104 | bytes 21178816 | tf_op jit(solution)/shard_map/dot_general | solution.py:123
  203.1 1.2 select_select_fusion
  204.2 5.5 %all-to-all-start.2 = ((bf16[8,2,64,256]{3,2,1,0:T(8,128)(2,1)}), bf16[8,2,64,256]{3,2,1,0:T(8,128)(2,1)S(1)}, u32[]{:S(2)}, u32[]{:S(2)}) async-start(bf16[8,2,64,256]{3,2,1,0:T(8,128)(2,1)} %bitcast.24), calls=%async_computation.3 | async-start | bytes 1048576 | tf_op jit(solution)/shard_map/all_to_all | solution.py:151
  211.4 13.1 %all-reduce = s32[104]{0:T(128)S(1)} all-reduce(s32[104]{0:T(128)S(1)} %dynamic-update-slice), channel_id=1, replica_groups=mesh['req'=8,'kv'=4] {'req'}, use_global_device_ids=true, to_apply=%add | all-reduce | flops 104 | bytes 832
  224.5 3.5 %all-to-all-start.3 = ((bf16[8,2,64,256]{3,2,1,0:T(8,128)(2,1)}), bf16[8,2,64,256]{3,2,1,0:T(8,128)(2,1)S(1)}, u32[]{:S(2)}, u32[]{:S(2)}) async-start(bf16[8,2,64,256]{3,2,1,0:T(8,128)(2,1)} %bitcast.27), calls=%async_computation.4 | async-start | bytes 1048576 | tf_op jit(solution)/shard_map/all_to_all | solution.py:152
  229.6 12.9 %all-to-all-done.3 = bf16[8,2,64,256]{3,2,1,0:T(8,128)(2,1)S(1)} async-done(((bf16[8,2,64,256]{3,2,1,0:T(8,128)(2,1)}), bf16[8,2,64,256]{3,2,1,0:T(8,128)(2,1)S(1)}, u32[]{:S(2)}, u32[]{:S(2)}) %all-to-all-start.3) | async-done | bytes 524320 | tf_op jit(solution)/shard_map/all_to_all | solution.py:152
  243.0 1.0 broadcast_select_fusion
  244.1 7.5 %reduce-scatter.2.cloned.1.call-done = f32[624,512]{1,0:T(8,128)} async-done(((f32[624,2048]{1,0:T(8,128)}), f32[624,512]{1,0:T(8,128)}) %reduce-scatter.2.cloned.1.call-update) | async-done | bytes 1277968 | tf_op jit(solution)/shard_map/reduce_scatter | solution.py:122
  251.6 2.7 %select_convert_fusion = bf16[624,512]{1,0:T(8,128)(2,1)} fusion(f32[624,512]{1,0:T(8,128)} %reduce-scatter.2.cloned.1.call-done, f32[624,2048]{1,0:T(8,128)} %copy-done.4, s32[]{:T(128)S(6)} %select_n.56, pred[624]{0:T(1024)(128)(4,1)S(1)} %lt.84), kind=kLoop, calls=%fused_computation.14 | loop fusion | flops 958464 | bytes 3195508 | tf_op jit(solution)/shard_map/convert_element_type | solution.py:131
  (88 shorter events, 9.4 us)
Async XLA Ops:
  7.2 62.7 %copy-start = (bf16[512,2048]{1,0:T(8,128)(2,1)S(1)}, bf16[512,2048]{1,0:T(8,128)(2,1)}, u32[]{:S(2)}) copy-start(bf16[512,2048]{1,0:T(8,128)(2,1)} %param.27) | copy-start | bytes 6291460
  7.2 44.9 %all-gather.2.cloned.1.call-start = ((), (), s32[]{:S(2)}) async-start(), calls=%async_computation.5 | async-start | bytes 3194880 | tf_op jit(solution)/shard_map/all_gather | solution.py:66
  13.6 9.8 %copy-start.15 = (s32[13]{0:T(128)S(1)}, s32[13]{0:T(128)}, u32[]{:S(2)}) copy-start(s32[13]{0:T(128)} %param.21) | copy-start | bytes 160
  13.6 9.8 %copy-start.9 = (bf16[13,16,1024]{2,1,0:T(8,128)(2,1)S(1)}, bf16[13,16,1024]{2,1,0:T(8,128)(2,1)}, u32[]{:S(2)}) copy-start(bf16[13,16,1024]{2,1,0:T(8,128)(2,1)} %param.33) | copy-start | bytes 1277956
  13.6 10.7 %copy-start.10 = (s32[13]{0:T(128)S(1)}, s32[13]{0:T(128)}, u32[]{:S(2)}) copy-start(s32[13]{0:T(128)} %param.20) | copy-start | bytes 160
  19.1 17.1 %all-to-all-start.1 = ((bf16[4,2,26624]{2,1,0:T(2,128)(2,1)}), bf16[4,2,26624]{2,1,0:T(2,128)(2,1)S(1)}, u32[]{:S(2)}, u32[]{:S(2)}) async-start(bf16[4,2,26624]{2,1,0:T(2,128)(2,1)} %reshape.333), calls=%async_computation.1 | async-start | bytes 851968 | tf_op jit(solution)/shard_map/all_to_all | solution.py:86
  36.2 15.1 %all-to-all-start = ((bf16[4,13,16,256]{3,2,1,0:T(8,128)(2,1)}), bf16[4,13,16,256]{3,2,1,0:T(8,128)(2,1)S(1)}, u32[]{:S(2)}, u32[]{:S(2)}) async-start(bf16[4,13,16,256]{3,2,1,0:T(8,128)(2,1)} %pad_maximum_fusion), calls=%async_computation | async-start | bytes 851968 | tf_op jit(solution)/shard_map/all_to_all | solution.py:88
  39.7 136.8 %all-reduce.3.cloned.1.call-start = ((), (), s32[]{:S(2)}) async-start(), calls=%async_computation.6 | async-start | bytes 10223616 | tf_op jit(solution)/shard_map/psum | solution.py:115
  51.3 3.3 %copy-start.13 = (f32[2048]{0:T(1024)S(1)}, f32[2048]{0:T(1024)}, u32[]{:S(2)}) copy-start(f32[2048]{0:T(1024)} %param.23) | copy-start | bytes 24580
  52.1 2.5 copy-start.2
  60.9 1.7 copy-start.3
  62.6 3.6 %copy-start.7 = (f32[13,48,128]{2,1,0:T(8,128)S(1)}, f32[13,48,128]{2,1,0:T(8,128)}, u32[]{:S(2)}) copy-start(f32[13,48,128]{2,1,0:T(8,128)} %get-tuple-element.21) | copy-start | bytes 958468
  62.6 3.6 %copy-start.8 = (f32[13,48,128]{2,1,0:T(8,128)S(1)}, f32[13,48,128]{2,1,0:T(8,128)}, u32[]{:S(2)}) copy-start(f32[13,48,128]{2,1,0:T(8,128)} %get-tuple-element.22) | copy-start | bytes 958468
  64.8 1.7 copy-start.5
  66.4 1.2 copy-start.12
  67.7 1.0 copy-start.6
  73.7 109.2 %copy-start.14 = (f32[2048]{0:T(1024)S(1)}, f32[2048]{0:T(1024)}, u32[]{:S(2)}) copy-start(f32[2048]{0:T(1024)} %param.28) | copy-start | bytes 24580
  73.7 177.9 %reduce-scatter.2.cloned.1.call-start = ((), (), s32[]{:S(2)}) async-start(), calls=%async_computation.7 | async-start | bytes 6389760 | tf_op jit(solution)/shard_map/reduce_scatter | solution.py:122
  176.5 6.4 %copy-start.11 = (bf16[2048,1024]{1,0:T(8,128)(2,1)S(1)}, bf16[2048,1024]{1,0:T(8,128)(2,1)}, u32[]{:S(2)}) copy-start(bf16[2048,1024]{1,0:T(8,128)(2,1)} %param.29) | copy-start | bytes 12582916
  180.6 2.3 copy-start.4
  200.8 0.7 copy-start.16
  201.9 8.0 %copy-start.17 = (u32[32]{0:T(128)S(1)}, u32[32]{0:T(128)}, u32[]{:S(2)}) copy-start(u32[32]{0:T(128)} %constant.89) | copy-start | bytes 388
  204.2 20.2 %all-to-all-start.2 = ((bf16[8,2,64,256]{3,2,1,0:T(8,128)(2,1)}), bf16[8,2,64,256]{3,2,1,0:T(8,128)(2,1)S(1)}, u32[]{:S(2)}, u32[]{:S(2)}) async-start(bf16[8,2,64,256]{3,2,1,0:T(8,128)(2,1)} %bitcast.24), calls=%async_computation.3 | async-start | bytes 1048576 | tf_op jit(solution)/shard_map/all_to_all | solution.py:151
  224.5 18.0 %all-to-all-start.3 = ((bf16[8,2,64,256]{3,2,1,0:T(8,128)(2,1)}), bf16[8,2,64,256]{3,2,1,0:T(8,128)(2,1)S(1)}, u32[]{:S(2)}, u32[]{:S(2)}) async-start(bf16[8,2,64,256]{3,2,1,0:T(8,128)(2,1)} %bitcast.27), calls=%async_computation.4 | async-start | bytes 1048576 | tf_op jit(solution)/shard_map/all_to_all | solution.py:152
  242.5 11.9 %copy-start.1 = (bf16[512,2048]{1,0:T(8,128)(2,1)S(1)}, bf16[512,2048]{1,0:T(8,128)(2,1)}, u32[]{:S(2)}) copy-start(bf16[512,2048]{1,0:T(8,128)(2,1)} %param.27) | copy-start | bytes 6291460
Sparse Core Ops, SparseCore 0:
  9.6 32.4 all-gather.1
  73.9 102.6 all-reduce.2
  200.9 50.6 reduce-scatter.1
